TPU v7x, 256 devices: a whole 4x4x8 slice. The times are simulated.
256 devices in a mesh: rad: 16 (over x, y_hi, core), azi: 16 (over z, y_lo).
Axes of the slice: x: 4, y: 4 (y_hi: 2, y_lo: 2; y = y_hi * 2 + y_lo), z: 8, core: 2. Of those that a mesh axis runs over, the one named last changes fastest.
Arguments:
- fields: float32 [5, 512, 256, 128], P(None, 'rad', 'azi'), may hold values from -6 to 6
- kappa: float32 [512, 256, 128], P('rad', 'azi'), may hold values from 0.01 to 0.1
- radial_speed: float32 [5, 512], P(None, 'rad'), may hold values from -0.5 to 0.5
- azimuth_speed: float32 [5, 512], P(None, 'rad'), may hold values from -0.5 to 0.5
- shifts: int32 [512], P('rad'), may hold values from 0 to 255
Outputs:
- advanced: float32 [5, 512, 256, 128], P(None, 'rad', 'azi')
All inputs are finite; a program needn't handle non-finite values.
Results may differ from a plain program's by a relative error of at most 0.00002.
Values sent between devices are 32-bit elements; how exact they have to be, the bound alone decides.
No kernel may reach another device: no remote copies, remote signals or barrier semaphores. Data moves between devices by JAX's collectives and lax.ppermute only.
A program may use at most 64 MiB of HBM per device.

v0:
```python
import jax
import jax.numpy as jnp
from jax import lax
from jax.sharding import PartitionSpec as P


def stencil(padded, kap, speed_r, speed_p):
    n_r = padded.shape[1] - 4
    n_p = padded.shape[2] - 4

    def tap(a, b):
        return padded[:, 2 + a : 2 + a + n_r, 2 + b : 2 + b + n_p, :]

    centre = tap(0, 0)
    height = centre.shape[3]
    zpad = jnp.pad(centre, ((0, 0), (0, 0), (0, 0), (2, 2)))

    def ztap(a):
        return zpad[:, :, :, 2 + a : 2 + a + height]

    first_r = (tap(-2, 0) - 8.0 * tap(-1, 0) + 8.0 * tap(1, 0) - tap(2, 0)) / 12.0
    first_p = (tap(0, -2) - 8.0 * tap(0, -1) + 8.0 * tap(0, 1) - tap(0, 2)) / 12.0
    second_r = (
        -tap(-2, 0) + 16.0 * tap(-1, 0) - 30.0 * centre + 16.0 * tap(1, 0) - tap(2, 0)
    ) / 12.0
    second_p = (
        -tap(0, -2) + 16.0 * tap(0, -1) - 30.0 * centre + 16.0 * tap(0, 1) - tap(0, 2)
    ) / 12.0
    second_z = (-ztap(-2) + 16.0 * ztap(-1) - 30.0 * centre + 16.0 * ztap(1) - ztap(2)) / 12.0
    return (
        -speed_r[:, :, None, None] * first_r
        - speed_p[:, :, None, None] * first_p
        + kap[None] * (second_r + second_p + second_z)
    )


def extend(cells, width):
    sectors, rings = (lax.axis_size("azi"), lax.axis_size("rad"))
    rows, cols = (cells.shape[-3], cells.shape[-2])
    left = lax.ppermute(
        cells[..., cols - width :, :], "azi", [(i, (i + 1) % sectors) for i in range(sectors)]
    )
    right = lax.ppermute(
        cells[..., :width, :], "azi", [((i + 1) % sectors, i) for i in range(sectors)]
    )
    above = lax.ppermute(
        cells[..., rows - width :, :, :], "rad", [(i, i + 1) for i in range(rings - 1)]
    )
    below = lax.ppermute(cells[..., :width, :, :], "rad", [(i + 1, i) for i in range(rings - 1)])
    wide = jnp.concatenate([left, cells, right], axis=-2)
    corners = [(0, 0)] * (cells.ndim - 2) + [(width, width), (0, 0)]
    return jnp.concatenate([jnp.pad(above, corners), wide, jnp.pad(below, corners)], axis=-3)


def heun_sections(field, kappa, speed_r, speed_p):
    first = field + stencil(extend(field, 2), kappa, speed_r, speed_p)
    return 0.5 * (field + first + stencil(extend(first, 2), kappa, speed_r, speed_p))


def shift_rows(half, shifts):
    peers = lax.axis_size("azi")
    rows = half.shape[1]
    per = rows // peers
    full = lax.all_to_all(half, "azi", 1, 2, tiled=True)
    length = full.shape[2]
    first = lax.axis_index("azi") * per
    mine = lax.dynamic_slice_in_dim(shifts, first, per)
    doubled = jnp.concatenate([full, full], axis=2)
    rolled = []
    for row in range(per):
        start = (length - mine[row] % length) % length
        rolled.append(lax.dynamic_slice_in_dim(doubled[:, row], start, length, axis=1))
    moved = jnp.stack(rolled, axis=1)
    return lax.all_to_all(moved, "azi", 2, 1, tiled=True)


def shards(fields, kappa, radial_speed, azimuth_speed, shifts):
    fcount = fields.shape[0]
    bounds = [0, (fcount + 1) // 2, fcount]
    groups = [
        (fields[lo:hi], radial_speed[lo:hi], azimuth_speed[lo:hi])
        for lo, hi in zip(bounds, bounds[1:])
    ]
    halves = [heun_sections(f, kappa, r, p) for f, r, p in groups]
    moved = [shift_rows(h, shifts) for h in halves]
    done = [heun_sections(m, kappa, r, p) for m, (_, r, p) in zip(moved, groups)]
    return jnp.concatenate(done, axis=0)


def solution(mesh):
    placed = (
        P(None, "rad", "azi", None),
        P("rad", "azi", None),
        P(None, "rad"),
        P(None, "rad"),
        P("rad"),
    )
    return jax.shard_map(
        shards, mesh=mesh, in_specs=placed, out_specs=P(None, "rad", "azi", None), check_vma=False
    )
```

profile of v0, /device:TPU:17, one launch (start us, length us, event | category | flops | bytes accessed | tf_op | source)
XLA Modules:
  0.0 201.3 jit_solution(1181467208800410658)
XLA Ops:
  5.4 3.6 %collective-permute-start.18 = (f32[2,32,2,128]{3,2,1,0:T(2,128)S(1)}, f32[2,32,2,128]{3,2,1,0:T(2,128)S(1)}, u32[]{:S(2)}, u32[]{:S(2)}) collective-permute-start(f32[2,32,2,128]{3,2,1,0:T(2,128)S(1)} %get-tuple-element.12), channel_id=1, source_target_pairs={{1,0},{2,1},{3,2},{4,3},{5,4},{6,5},{7,6},{8,7},{9,8},{10,9},{11,1... | collective-permute-start | bytes 196616 | tf_op jit(solution)/shard_map/ppermute | solution.py:43
  9.7 4.0 %collective-permute-start.16 = (f32[2,2,16,128]{3,2,1,0:T(8,128)S(1)}, f32[2,2,16,128]{3,2,1,0:T(8,128)S(1)}, u32[]{:S(2)}, u32[]{:S(2)}) collective-permute-start(f32[2,2,16,128]{3,2,1,0:T(8,128)S(1)} %get-tuple-element.9), channel_id=1, source_target_pairs={{0,16},{16,32},{32,48},{48,64},{64,80},{80,96},{96,112},{112,128},... | collective-permute-start | bytes 98312 | tf_op jit(solution)/shard_map/ppermute | solution.py:46
  17.7 2.4 %collective-permute-start.2 = (f32[3,32,2,128]{3,2,1,0:T(2,128)S(1)}, f32[3,32,2,128]{3,2,1,0:T(2,128)S(1)}, u32[]{:S(2)}, u32[]{:S(2)}) collective-permute-start(f32[3,32,2,128]{3,2,1,0:T(2,128)S(1)} %get-tuple-element.8), channel_id=1, source_target_pairs={{1,0},{2,1},{3,2},{4,3},{5,4},{6,5},{7,6},{8,7},{9,8},{10,9},{11,1... | collective-permute-start | bytes 294920 | tf_op jit(solution)/shard_map/ppermute | solution.py:43
  21.4 4.4 %collective-permute-start = (f32[3,2,16,128]{3,2,1,0:T(8,128)S(1)}, f32[3,2,16,128]{3,2,1,0:T(8,128)S(1)}, u32[]{:S(2)}, u32[]{:S(2)}) collective-permute-start(f32[3,2,16,128]{3,2,1,0:T(8,128)S(1)} %get-tuple-element.5), channel_id=1, source_target_pairs={{0,16},{16,32},{32,48},{48,64},{64,80},{80,96},{96,112},{112,128},... | collective-permute-start | bytes 147464 | tf_op jit(solution)/shard_map/ppermute | solution.py:46
  29.6 3.2 %collective-permute-start.22 = (f32[2,32,2,128]{3,2,1,0:T(2,128)S(1)}, f32[2,32,2,128]{3,2,1,0:T(2,128)S(1)}, u32[]{:S(2)}, u32[]{:S(2)}) collective-permute-start(f32[2,32,2,128]{3,2,1,0:T(2,128)S(1)} %get-tuple-element.56), channel_id=1, source_target_pairs={{1,0},{2,1},{3,2},{4,3},{5,4},{6,5},{7,6},{8,7},{9,8},{10,9},{11,1... | collective-permute-start | bytes 196616 | tf_op jit(solution)/shard_map/ppermute | solution.py:43
  33.6 5.8 %collective-permute-start.20 = (f32[2,2,16,128]{3,2,1,0:T(8,128)S(1)}, f32[2,2,16,128]{3,2,1,0:T(8,128)S(1)}, u32[]{:S(2)}, u32[]{:S(2)}) collective-permute-start(f32[2,2,16,128]{3,2,1,0:T(8,128)S(1)} %get-tuple-element.53), channel_id=1, source_target_pairs={{0,16},{16,32},{32,48},{48,64},{64,80},{80,96},{96,112},{112,128},... | collective-permute-start | bytes 98312 | tf_op jit(solution)/shard_map/ppermute | solution.py:46
  43.9 3.6 %collective-permute-start.6 = (f32[3,32,2,128]{3,2,1,0:T(2,128)S(1)}, f32[3,32,2,128]{3,2,1,0:T(2,128)S(1)}, u32[]{:S(2)}, u32[]{:S(2)}) collective-permute-start(f32[3,32,2,128]{3,2,1,0:T(2,128)S(1)} %get-tuple-element.34), channel_id=1, source_target_pairs={{1,0},{2,1},{3,2},{4,3},{5,4},{6,5},{7,6},{8,7},{9,8},{10,9},{11,1... | collective-permute-start | bytes 294920 | tf_op jit(solution)/shard_map/ppermute | solution.py:43
  49.8 5.5 %all-to-all-start.2 = ((f32[2,32,16,128]{3,2,0,1:T(8,128)}), f32[2,32,16,128]{3,2,0,1:T(8,128)S(1)}, u32[]{:S(2)}, u32[]{:S(2)}) async-start(f32[2,32,16,128]{3,2,0,1:T(8,128)} %copy.16), calls=%async_computation.2 | async-start | bytes 1048576 | tf_op jit(solution)/shard_map/all_to_all | solution.py:64
  55.3 6.9 %collective-permute-start.4 = (f32[3,2,16,128]{3,2,1,0:T(8,128)S(1)}, f32[3,2,16,128]{3,2,1,0:T(8,128)S(1)}, u32[]{:S(2)}, u32[]{:S(2)}) collective-permute-start(f32[3,2,16,128]{3,2,1,0:T(8,128)S(1)} %get-tuple-element.31), channel_id=1, source_target_pairs={{0,16},{16,32},{32,48},{48,64},{64,80},{80,96},{96,112},{112,128},... | collective-permute-start | bytes 147464 | tf_op jit(solution)/shard_map/ppermute | solution.py:46
  64.3 6.0 %collective-permute-done.7 = f32[3,2,16,128]{3,2,1,0:T(8,128)S(1)} collective-permute-done((f32[3,2,16,128]{3,2,1,0:T(8,128)S(1)}, f32[3,2,16,128]{3,2,1,0:T(8,128)S(1)}, u32[]{:S(2)}, u32[]{:S(2)}) %collective-permute-start.7) | collective-permute-done | bytes 49184 | tf_op jit(solution)/shard_map/ppermute | solution.py:49
  73.7 8.1 %all-to-all-start = ((f32[3,32,16,128]{3,2,0,1:T(8,128)}), f32[3,32,16,128]{3,2,0,1:T(8,128)S(1)}, u32[]{:S(2)}, u32[]{:S(2)}) async-start(f32[3,32,16,128]{3,2,0,1:T(8,128)} %copy.10), calls=%async_computation | async-start | bytes 1572864 | tf_op jit(solution)/shard_map/all_to_all | solution.py:64
  87.8 14.5 %all-to-all-done = f32[3,32,16,128]{3,2,0,1:T(8,128)S(1)} async-done(((f32[3,32,16,128]{3,2,0,1:T(8,128)}), f32[3,32,16,128]{3,2,0,1:T(8,128)S(1)}, u32[]{:S(2)}, u32[]{:S(2)}) %all-to-all-start) | async-done | bytes 786464 | tf_op jit(solution)/shard_map/all_to_all | solution.py:64
  102.3 3.6 %all-to-all-start.3 = ((f32[2,2,256,128]{3,1,0,2:T(2,128)}), f32[2,2,256,128]{3,1,0,2:T(2,128)S(1)}, u32[]{:S(2)}, u32[]{:S(2)}) async-start(f32[2,2,256,128]{3,1,0,2:T(2,128)} %copy.19), calls=%async_computation.3 | async-start | bytes 1048576 | tf_op jit(solution)/shard_map/all_to_all | solution.py:74
  107.9 14.7 %all-to-all-done.3 = f32[2,2,256,128]{3,1,0,2:T(2,128)S(1)} async-done(((f32[2,2,256,128]{3,1,0,2:T(2,128)}), f32[2,2,256,128]{3,1,0,2:T(2,128)S(1)}, u32[]{:S(2)}, u32[]{:S(2)}) %all-to-all-start.3) | async-done | bytes 524320 | tf_op jit(solution)/shard_map/all_to_all | solution.py:74
  122.5 3.7 %all-to-all-start.1 = ((f32[3,2,256,128]{3,1,0,2:T(2,128)}), f32[3,2,256,128]{3,1,0,2:T(2,128)S(1)}, u32[]{:S(2)}, u32[]{:S(2)}) async-start(f32[3,2,256,128]{3,1,0,2:T(2,128)} %copy.13), calls=%async_computation.1 | async-start | bytes 1572864 | tf_op jit(solution)/shard_map/all_to_all | solution.py:74
  130.1 7.4 %collective-permute-start.24 = (f32[2,2,16,128]{3,2,1,0:T(8,128)S(1)}, f32[2,2,16,128]{3,2,1,0:T(8,128)S(1)}, u32[]{:S(2)}, u32[]{:S(2)}) collective-permute-start(f32[2,2,16,128]{3,2,1,0:T(8,128)S(1)} %get-tuple-element.47), channel_id=1, source_target_pairs={{0,16},{16,32},{32,48},{48,64},{64,80},{80,96},{96,112},{112,128},... | collective-permute-start | bytes 98312 | tf_op jit(solution)/shard_map/ppermute | solution.py:46
  139.4 6.0 %collective-permute-done.27 = f32[2,2,16,128]{3,2,1,0:T(8,128)S(1)} collective-permute-done((f32[2,2,16,128]{3,2,1,0:T(8,128)S(1)}, f32[2,2,16,128]{3,2,1,0:T(8,128)S(1)}, u32[]{:S(2)}, u32[]{:S(2)}) %collective-permute-start.27) | collective-permute-done | bytes 32800 | tf_op jit(solution)/shard_map/ppermute | solution.py:49
  149.0 2.3 %collective-permute-start.30 = (f32[2,32,2,128]{3,2,1,0:T(2,128)S(1)}, f32[2,32,2,128]{3,2,1,0:T(2,128)S(1)}, u32[]{:S(2)}, u32[]{:S(2)}) collective-permute-start(f32[2,32,2,128]{3,2,1,0:T(2,128)S(1)} %get-tuple-element.46), channel_id=1, source_target_pairs={{1,0},{2,1},{3,2},{4,3},{5,4},{6,5},{7,6},{8,7},{9,8},{10,9},{11,1... | collective-permute-start | bytes 196616 | tf_op jit(solution)/shard_map/ppermute | solution.py:43
  151.4 8.4 %collective-permute-start.28 = (f32[2,2,16,128]{3,2,1,0:T(8,128)S(1)}, f32[2,2,16,128]{3,2,1,0:T(8,128)S(1)}, u32[]{:S(2)}, u32[]{:S(2)}) collective-permute-start(f32[2,2,16,128]{3,2,1,0:T(8,128)S(1)} %get-tuple-element.43), channel_id=1, source_target_pairs={{0,16},{16,32},{32,48},{48,64},{64,80},{80,96},{96,112},{112,128},... | collective-permute-start | bytes 98312 | tf_op jit(solution)/shard_map/ppermute | solution.py:46
  163.6 3.9 %collective-permute-done.31 = f32[2,2,16,128]{3,2,1,0:T(8,128)S(1)} collective-permute-done((f32[2,2,16,128]{3,2,1,0:T(8,128)S(1)}, f32[2,2,16,128]{3,2,1,0:T(8,128)S(1)}, u32[]{:S(2)}, u32[]{:S(2)}) %collective-permute-start.31) | collective-permute-done | bytes 32800 | tf_op jit(solution)/shard_map/ppermute | solution.py:49
  169.4 6.3 %collective-permute-start.8 = (f32[3,2,16,128]{3,2,1,0:T(8,128)S(1)}, f32[3,2,16,128]{3,2,1,0:T(8,128)S(1)}, u32[]{:S(2)}, u32[]{:S(2)}) collective-permute-start(f32[3,2,16,128]{3,2,1,0:T(8,128)S(1)} %get-tuple-element.25), channel_id=1, source_target_pairs={{0,16},{16,32},{32,48},{48,64},{64,80},{80,96},{96,112},{112,128},... | collective-permute-start | bytes 147464 | tf_op jit(solution)/shard_map/ppermute | solution.py:46
  179.1 3.6 %collective-permute-start.14 = (f32[3,32,2,128]{3,2,1,0:T(2,128)S(1)}, f32[3,32,2,128]{3,2,1,0:T(2,128)S(1)}, u32[]{:S(2)}, u32[]{:S(2)}) collective-permute-start(f32[3,32,2,128]{3,2,1,0:T(2,128)S(1)} %get-tuple-element.24), channel_id=1, source_target_pairs={{1,0},{2,1},{3,2},{4,3},{5,4},{6,5},{7,6},{8,7},{9,8},{10,9},{11,1... | collective-permute-start | bytes 294920 | tf_op jit(solution)/shard_map/ppermute | solution.py:43
  182.7 7.2 %collective-permute-start.12 = (f32[3,2,16,128]{3,2,1,0:T(8,128)S(1)}, f32[3,2,16,128]{3,2,1,0:T(8,128)S(1)}, u32[]{:S(2)}, u32[]{:S(2)}) collective-permute-start(f32[3,2,16,128]{3,2,1,0:T(8,128)S(1)} %get-tuple-element.21), channel_id=1, source_target_pairs={{0,16},{16,32},{32,48},{48,64},{64,80},{80,96},{96,112},{112,128},... | collective-permute-start | bytes 147464 | tf_op jit(solution)/shard_map/ppermute | solution.py:46
  193.1 4.6 %collective-permute-done.15 = f32[3,2,16,128]{3,2,1,0:T(8,128)S(1)} collective-permute-done((f32[3,2,16,128]{3,2,1,0:T(8,128)S(1)}, f32[3,2,16,128]{3,2,1,0:T(8,128)S(1)}, u32[]{:S(2)}, u32[]{:S(2)}) %collective-permute-start.15) | collective-permute-done | bytes 49184 | tf_op jit(solution)/shard_map/ppermute | solution.py:49
  (114 shorter events, 57.2 us)
Async XLA Ops:
  1.3 38.2 %collective-permute-start.1 = (f32[3,32,2,128]{3,2,1,0:T(2,128)S(1)}, f32[3,32,2,128]{3,2,1,0:T(2,128)S(1)}, u32[]{:S(2)}, u32[]{:S(2)}) collective-permute-start(f32[3,32,2,128]{3,2,1,0:T(2,128)S(1)} %get-tuple-element.7), channel_id=1, source_target_pairs={{0,1},{1,2},{2,3},{3,4},{4,5},{5,6},{6,7},{7,8},{8,9},{9,10},{10,1... | collective-permute-start | bytes 294920 | tf_op jit(solution)/shard_map/ppermute | solution.py:40
  3.5 22.3 %collective-permute-start.17 = (f32[2,32,2,128]{3,2,1,0:T(2,128)S(1)}, f32[2,32,2,128]{3,2,1,0:T(2,128)S(1)}, u32[]{:S(2)}, u32[]{:S(2)}) collective-permute-start(f32[2,32,2,128]{3,2,1,0:T(2,128)S(1)} %get-tuple-element.11), channel_id=1, source_target_pairs={{0,1},{1,2},{2,3},{3,4},{4,5},{5,6},{6,7},{7,8},{8,9},{9,10},{10,1... | collective-permute-start | bytes 196616 | tf_op jit(solution)/shard_map/ppermute | solution.py:40
  5.4 22.4 %collective-permute-start.18 = (f32[2,32,2,128]{3,2,1,0:T(2,128)S(1)}, f32[2,32,2,128]{3,2,1,0:T(2,128)S(1)}, u32[]{:S(2)}, u32[]{:S(2)}) collective-permute-start(f32[2,32,2,128]{3,2,1,0:T(2,128)S(1)} %get-tuple-element.12), channel_id=1, source_target_pairs={{1,0},{2,1},{3,2},{4,3},{5,4},{6,5},{7,6},{8,7},{9,8},{10,9},{11,1... | collective-permute-start | bytes 196616 | tf_op jit(solution)/shard_map/ppermute | solution.py:43
  17.7 23.7 %collective-permute-start.2 = (f32[3,32,2,128]{3,2,1,0:T(2,128)S(1)}, f32[3,32,2,128]{3,2,1,0:T(2,128)S(1)}, u32[]{:S(2)}, u32[]{:S(2)}) collective-permute-start(f32[3,32,2,128]{3,2,1,0:T(2,128)S(1)} %get-tuple-element.8), channel_id=1, source_target_pairs={{1,0},{2,1},{3,2},{4,3},{5,4},{6,5},{7,6},{8,7},{9,8},{10,9},{11,1... | collective-permute-start | bytes 294920 | tf_op jit(solution)/shard_map/ppermute | solution.py:43
  29.2 18.3 %collective-permute-start.21 = (f32[2,32,2,128]{3,2,1,0:T(2,128)S(1)}, f32[2,32,2,128]{3,2,1,0:T(2,128)S(1)}, u32[]{:S(2)}, u32[]{:S(2)}) collective-permute-start(f32[2,32,2,128]{3,2,1,0:T(2,128)S(1)} %get-tuple-element.55), channel_id=1, source_target_pairs={{0,1},{1,2},{2,3},{3,4},{4,5},{5,6},{6,7},{7,8},{8,9},{9,10},{10,1... | collective-permute-start | bytes 196616 | tf_op jit(solution)/shard_map/ppermute | solution.py:40
  29.6 17.9 %collective-permute-start.22 = (f32[2,32,2,128]{3,2,1,0:T(2,128)S(1)}, f32[2,32,2,128]{3,2,1,0:T(2,128)S(1)}, u32[]{:S(2)}, u32[]{:S(2)}) collective-permute-start(f32[2,32,2,128]{3,2,1,0:T(2,128)S(1)} %get-tuple-element.56), channel_id=1, source_target_pairs={{1,0},{2,1},{3,2},{4,3},{5,4},{6,5},{7,6},{8,7},{9,8},{10,9},{11,1... | collective-permute-start | bytes 196616 | tf_op jit(solution)/shard_map/ppermute | solution.py:43
  33.6 10.3 %collective-permute-start.20 = (f32[2,2,16,128]{3,2,1,0:T(8,128)S(1)}, f32[2,2,16,128]{3,2,1,0:T(8,128)S(1)}, u32[]{:S(2)}, u32[]{:S(2)}) collective-permute-start(f32[2,2,16,128]{3,2,1,0:T(8,128)S(1)} %get-tuple-element.53), channel_id=1, source_target_pairs={{0,16},{16,32},{32,48},{48,64},{64,80},{80,96},{96,112},{112,128},... | collective-permute-start | bytes 98312 | tf_op jit(solution)/shard_map/ppermute | solution.py:46
  43.8 26.5 %collective-permute-start.5 = (f32[3,32,2,128]{3,2,1,0:T(2,128)S(1)}, f32[3,32,2,128]{3,2,1,0:T(2,128)S(1)}, u32[]{:S(2)}, u32[]{:S(2)}) collective-permute-start(f32[3,32,2,128]{3,2,1,0:T(2,128)S(1)} %get-tuple-element.33), channel_id=1, source_target_pairs={{0,1},{1,2},{2,3},{3,4},{4,5},{5,6},{6,7},{7,8},{8,9},{9,10},{10,1... | collective-permute-start | bytes 294920 | tf_op jit(solution)/shard_map/ppermute | solution.py:40
  43.9 26.4 %collective-permute-start.6 = (f32[3,32,2,128]{3,2,1,0:T(2,128)S(1)}, f32[3,32,2,128]{3,2,1,0:T(2,128)S(1)}, u32[]{:S(2)}, u32[]{:S(2)}) collective-permute-start(f32[3,32,2,128]{3,2,1,0:T(2,128)S(1)} %get-tuple-element.34), channel_id=1, source_target_pairs={{1,0},{2,1},{3,2},{4,3},{5,4},{6,5},{7,6},{8,7},{9,8},{10,9},{11,1... | collective-permute-start | bytes 294920 | tf_op jit(solution)/shard_map/ppermute | solution.py:43
  49.8 23.8 %all-to-all-start.2 = ((f32[2,32,16,128]{3,2,0,1:T(8,128)}), f32[2,32,16,128]{3,2,0,1:T(8,128)S(1)}, u32[]{:S(2)}, u32[]{:S(2)}) async-start(f32[2,32,16,128]{3,2,0,1:T(8,128)} %copy.16), calls=%async_computation.2 | async-start | bytes 1048576 | tf_op jit(solution)/shard_map/all_to_all | solution.py:64
  73.7 28.7 %all-to-all-start = ((f32[3,32,16,128]{3,2,0,1:T(8,128)}), f32[3,32,16,128]{3,2,0,1:T(8,128)S(1)}, u32[]{:S(2)}, u32[]{:S(2)}) async-start(f32[3,32,16,128]{3,2,0,1:T(8,128)} %copy.10), calls=%async_computation | async-start | bytes 1572864 | tf_op jit(solution)/shard_map/all_to_all | solution.py:64
  102.3 20.2 %all-to-all-start.3 = ((f32[2,2,256,128]{3,1,0,2:T(2,128)}), f32[2,2,256,128]{3,1,0,2:T(2,128)S(1)}, u32[]{:S(2)}, u32[]{:S(2)}) async-start(f32[2,2,256,128]{3,1,0,2:T(2,128)} %copy.19), calls=%async_computation.3 | async-start | bytes 1048576 | tf_op jit(solution)/shard_map/all_to_all | solution.py:74
  122.5 39.2 %all-to-all-start.1 = ((f32[3,2,256,128]{3,1,0,2:T(2,128)}), f32[3,2,256,128]{3,1,0,2:T(2,128)S(1)}, u32[]{:S(2)}, u32[]{:S(2)}) async-start(f32[3,2,256,128]{3,1,0,2:T(2,128)} %copy.13), calls=%async_computation.1 | async-start | bytes 1572864 | tf_op jit(solution)/shard_map/all_to_all | solution.py:74
  126.4 19.8 %collective-permute-start.25 = (f32[2,32,2,128]{3,2,1,0:T(2,128)S(1)}, f32[2,32,2,128]{3,2,1,0:T(2,128)S(1)}, u32[]{:S(2)}, u32[]{:S(2)}) collective-permute-start(f32[2,32,2,128]{3,2,1,0:T(2,128)S(1)} %get-tuple-element.49), channel_id=1, source_target_pairs={{0,1},{1,2},{2,3},{3,4},{4,5},{5,6},{6,7},{7,8},{8,9},{9,10},{10,1... | collective-permute-start | bytes 196616 | tf_op jit(solution)/shard_map/ppermute | solution.py:40
  127.8 18.4 %collective-permute-start.26 = (f32[2,32,2,128]{3,2,1,0:T(2,128)S(1)}, f32[2,32,2,128]{3,2,1,0:T(2,128)S(1)}, u32[]{:S(2)}, u32[]{:S(2)}) collective-permute-start(f32[2,32,2,128]{3,2,1,0:T(2,128)S(1)} %get-tuple-element.50), channel_id=1, source_target_pairs={{1,0},{2,1},{3,2},{4,3},{5,4},{6,5},{7,6},{8,7},{9,8},{10,9},{11,1... | collective-permute-start | bytes 196616 | tf_op jit(solution)/shard_map/ppermute | solution.py:43
  130.1 9.4 %collective-permute-start.24 = (f32[2,2,16,128]{3,2,1,0:T(8,128)S(1)}, f32[2,2,16,128]{3,2,1,0:T(8,128)S(1)}, u32[]{:S(2)}, u32[]{:S(2)}) collective-permute-start(f32[2,2,16,128]{3,2,1,0:T(8,128)S(1)} %get-tuple-element.47), channel_id=1, source_target_pairs={{0,16},{16,32},{32,48},{48,64},{64,80},{80,96},{96,112},{112,128},... | collective-permute-start | bytes 98312 | tf_op jit(solution)/shard_map/ppermute | solution.py:46
  147.7 21.7 %collective-permute-start.29 = (f32[2,32,2,128]{3,2,1,0:T(2,128)S(1)}, f32[2,32,2,128]{3,2,1,0:T(2,128)S(1)}, u32[]{:S(2)}, u32[]{:S(2)}) collective-permute-start(f32[2,32,2,128]{3,2,1,0:T(2,128)S(1)} %get-tuple-element.45), channel_id=1, source_target_pairs={{0,1},{1,2},{2,3},{3,4},{4,5},{5,6},{6,7},{7,8},{8,9},{9,10},{10,1... | collective-permute-start | bytes 196616 | tf_op jit(solution)/shard_map/ppermute | solution.py:40
  149.0 26.6 %collective-permute-start.30 = (f32[2,32,2,128]{3,2,1,0:T(2,128)S(1)}, f32[2,32,2,128]{3,2,1,0:T(2,128)S(1)}, u32[]{:S(2)}, u32[]{:S(2)}) collective-permute-start(f32[2,32,2,128]{3,2,1,0:T(2,128)S(1)} %get-tuple-element.46), channel_id=1, source_target_pairs={{1,0},{2,1},{3,2},{4,3},{5,4},{6,5},{7,6},{8,7},{9,8},{10,9},{11,1... | collective-permute-start | bytes 196616 | tf_op jit(solution)/shard_map/ppermute | solution.py:43
  151.4 11.1 %collective-permute-start.28 = (f32[2,2,16,128]{3,2,1,0:T(8,128)S(1)}, f32[2,2,16,128]{3,2,1,0:T(8,128)S(1)}, u32[]{:S(2)}, u32[]{:S(2)}) collective-permute-start(f32[2,2,16,128]{3,2,1,0:T(8,128)S(1)} %get-tuple-element.43), channel_id=1, source_target_pairs={{0,16},{16,32},{32,48},{48,64},{64,80},{80,96},{96,112},{112,128},... | collective-permute-start | bytes 98312 | tf_op jit(solution)/shard_map/ppermute | solution.py:46
  162.0 14.6 %collective-permute-start.10 = (f32[3,32,2,128]{3,2,1,0:T(2,128)S(1)}, f32[3,32,2,128]{3,2,1,0:T(2,128)S(1)}, u32[]{:S(2)}, u32[]{:S(2)}) collective-permute-start(f32[3,32,2,128]{3,2,1,0:T(2,128)S(1)} %get-tuple-element.28), channel_id=1, source_target_pairs={{1,0},{2,1},{3,2},{4,3},{5,4},{6,5},{7,6},{8,7},{9,8},{10,9},{11,1... | collective-permute-start | bytes 294920 | tf_op jit(solution)/shard_map/ppermute | solution.py:43
  162.4 14.2 %collective-permute-start.9 = (f32[3,32,2,128]{3,2,1,0:T(2,128)S(1)}, f32[3,32,2,128]{3,2,1,0:T(2,128)S(1)}, u32[]{:S(2)}, u32[]{:S(2)}) collective-permute-start(f32[3,32,2,128]{3,2,1,0:T(2,128)S(1)} %get-tuple-element.27), channel_id=1, source_target_pairs={{0,1},{1,2},{2,3},{3,4},{4,5},{5,6},{6,7},{7,8},{8,9},{9,10},{10,1... | collective-permute-start | bytes 294920 | tf_op jit(solution)/shard_map/ppermute | solution.py:40
  179.0 18.7 %collective-permute-start.13 = (f32[3,32,2,128]{3,2,1,0:T(2,128)S(1)}, f32[3,32,2,128]{3,2,1,0:T(2,128)S(1)}, u32[]{:S(2)}, u32[]{:S(2)}) collective-permute-start(f32[3,32,2,128]{3,2,1,0:T(2,128)S(1)} %get-tuple-element.23), channel_id=1, source_target_pairs={{0,1},{1,2},{2,3},{3,4},{4,5},{5,6},{6,7},{7,8},{8,9},{9,10},{10,1... | collective-permute-start | bytes 294920 | tf_op jit(solution)/shard_map/ppermute | solution.py:40
  179.1 18.6 %collective-permute-start.14 = (f32[3,32,2,128]{3,2,1,0:T(2,128)S(1)}, f32[3,32,2,128]{3,2,1,0:T(2,128)S(1)}, u32[]{:S(2)}, u32[]{:S(2)}) collective-permute-start(f32[3,32,2,128]{3,2,1,0:T(2,128)S(1)} %get-tuple-element.24), channel_id=1, source_target_pairs={{1,0},{2,1},{3,2},{4,3},{5,4},{6,5},{7,6},{8,7},{9,8},{10,9},{11,1... | collective-permute-start | bytes 294920 | tf_op jit(solution)/shard_map/ppermute | solution.py:43
  182.7 10.4 %collective-permute-start.12 = (f32[3,2,16,128]{3,2,1,0:T(8,128)S(1)}, f32[3,2,16,128]{3,2,1,0:T(8,128)S(1)}, u32[]{:S(2)}, u32[]{:S(2)}) collective-permute-start(f32[3,2,16,128]{3,2,1,0:T(8,128)S(1)} %get-tuple-element.21), channel_id=1, source_target_pairs={{0,16},{16,32},{32,48},{48,64},{64,80},{80,96},{96,112},{112,128},... | collective-permute-start | bytes 147464 | tf_op jit(solution)/shard_map/ppermute | solution.py:46
  (16 other events, 157.3 us)
where the time goes:
time: 202 us; the launch traced here: 201 us
  starting transfers between devices  116 us (57%)
  waiting for transfers between devices  53.3 us (26%)
  other arithmetic  17.7 us (9%)
  local copies, waits for them, and re-layouts  10.2 us (5%)
  between operations  4.4 us (2%)
    ppermute x8, starting transfers between devices, extend(): lax.ppermute(cells[..., rows - width:, :, :], 'rad', [(i, i + 1) for i in...  50.5 us
    ppermute x8, waiting for transfers between devices, extend(): lax.ppermute(cells[..., :width, :, :], 'rad', [(i + 1, i) for i in range(...  22.5 us
    ppermute x8, starting transfers between devices, extend(): lax.ppermute(cells[..., :width, :], 'azi', [((i + 1) % sectors, i) for i...  21.3 us
    ppermute x8, starting transfers between devices, extend(): lax.ppermute(cells[..., :width, :, :], 'rad', [(i + 1, i) for i in range(...  15.5 us
    all_to_all x2, waiting for transfers between devices, shift_rows(): return lax.all_to_all(moved, 'azi', 2, 1, tiled=True)  14.7 us
    all_to_all x2, waiting for transfers between devices, shift_rows(): full = lax.all_to_all(half, 'azi', 1, 2, tiled=True)  14.5 us
    all_to_all x2, starting transfers between devices, shift_rows(): full = lax.all_to_all(half, 'azi', 1, 2, tiled=True)  13.6 us
    ppermute x8, starting transfers between devices, extend(): lax.ppermute(cells[..., cols - width:, :], 'azi', [(i, (i + 1) % sectors)...  7.44 us
  transfers between devices with their start and end apart: 36, of which 10 were waited for; matrix products, arithmetic and copies ran while one was open for 10% of the time, Pallas kernels for 0%

commit v1 on v0

--- a/solution.py
+++ b/solution.py
@@ -2,6 +2,18 @@
 import jax.numpy as jnp
 from jax import lax
 from jax.sharding import PartitionSpec as P
+
+
+def do_limits_all(x_in, group_axis):
+    return jnp.concatenate(
+        lax.all_to_all(
+            jnp.stack(jnp.split(x_in, lax.axis_size(group_axis), axis=1)),
+            axis_name=group_axis,
+            split_axis=0,
+            concat_axis=0,
+        ),
+        axis=2,
+    )
 
 
 def stencil(padded, kap, speed_r, speed_p):
@@ -61,7 +73,7 @@
     peers = lax.axis_size("azi")
     rows = half.shape[1]
     per = rows // peers
-    full = lax.all_to_all(half, "azi", 1, 2, tiled=True)
+    full = do_limits_all(half, "azi")
     length = full.shape[2]
     first = lax.axis_index("azi") * per
     mine = lax.dynamic_slice_in_dim(shifts, first, per)

time: 202 us -> 212 us (1.050)
  the two profiles are of different devices: /device:TPU:17 before, /device:TPU:1 now
where the time goes in v1:
time: 212 us; the launch traced here: 211 us
  starting transfers between devices  115 us (54%)
  waiting for transfers between devices  46.2 us (22%)
  local copies, waits for them, and re-layouts  28.2 us (13%)
  other arithmetic  17.7 us (8%)
  between operations  4.47 us (2%)
    ppermute x8, starting transfers between devices, extend(): lax.ppermute(cells[..., rows - width:, :, :], 'rad', [(i, i + 1) for i in...  52.1 us
    ppermute x8, starting transfers between devices, extend(): lax.ppermute(cells[..., :width, :], 'azi', [((i + 1) % sectors, i) for i...  20.9 us
    unnamed x38, local copies, waits for them, and re-layouts  18.5 us
    all_to_all x2, waiting for transfers between devices, do_limits_all(): lax.all_to_all(jnp.stack(jnp.split(x_in, lax.axis_size(group_axis), axis=...  16.1 us
    ppermute x8, starting transfers between devices, extend(): lax.ppermute(cells[..., :width, :, :], 'rad', [(i + 1, i) for i in range(...  15.4 us
    all_to_all x2, waiting for transfers between devices, shift_rows(): return lax.all_to_all(moved, 'azi', 2, 1, tiled=True)  14.8 us
    ppermute x8, waiting for transfers between devices, extend(): lax.ppermute(cells[..., :width, :, :], 'rad', [(i + 1, i) for i in range(...  14.5 us
    all_to_all x2, starting transfers between devices, do_limits_all(): lax.all_to_all(jnp.stack(jnp.split(x_in, lax.axis_size(group_axis), axis=...  11.3 us
  transfers between devices with their start and end apart: 36, of which 9 were waited for; matrix products, arithmetic and copies ran while one was open for 18% of the time, Pallas kernels for 0%

profile of v1, /device:TPU:1, one launch (start us, length us, event | category | flops | bytes accessed | tf_op | source)
XLA Modules:
  0.0 211.3 jit_solution(5706859375521280054)
XLA Ops:
  1.3 2.2 %collective-permute-start.1 = (f32[3,32,2,128]{3,2,1,0:T(2,128)S(1)}, f32[3,32,2,128]{3,2,1,0:T(2,128)S(1)}, u32[]{:S(2)}, u32[]{:S(2)}) collective-permute-start(f32[3,32,2,128]{3,2,1,0:T(2,128)S(1)} %get-tuple-element.7), channel_id=1, source_target_pairs={{0,1},{1,2},{2,3},{3,4},{4,5},{5,6},{6,7},{7,8},{8,9},{9,10},{10,1... | collective-permute-start | bytes 294920 | tf_op jit(solution)/shard_map/ppermute | solution.py:52
  6.2 3.9 %collective-permute-start.18 = (f32[2,32,2,128]{3,2,1,0:T(2,128)S(1)}, f32[2,32,2,128]{3,2,1,0:T(2,128)S(1)}, u32[]{:S(2)}, u32[]{:S(2)}) collective-permute-start(f32[2,32,2,128]{3,2,1,0:T(2,128)S(1)} %get-tuple-element.12), channel_id=1, source_target_pairs={{1,0},{2,1},{3,2},{4,3},{5,4},{6,5},{7,6},{8,7},{9,8},{10,9},{11,1... | collective-permute-start | bytes 196616 | tf_op jit(solution)/shard_map/ppermute | solution.py:55
  10.8 5.4 %collective-permute-start.16 = (f32[2,2,16,128]{3,2,1,0:T(8,128)S(1)}, f32[2,2,16,128]{3,2,1,0:T(8,128)S(1)}, u32[]{:S(2)}, u32[]{:S(2)}) collective-permute-start(f32[2,2,16,128]{3,2,1,0:T(8,128)S(1)} %get-tuple-element.9), channel_id=1, source_target_pairs={{0,16},{16,32},{32,48},{48,64},{64,80},{80,96},{96,112},{112,128},... | collective-permute-start | bytes 98312 | tf_op jit(solution)/shard_map/ppermute | solution.py:58
  23.5 3.9 %collective-permute-start = (f32[3,2,16,128]{3,2,1,0:T(8,128)S(1)}, f32[3,2,16,128]{3,2,1,0:T(8,128)S(1)}, u32[]{:S(2)}, u32[]{:S(2)}) collective-permute-start(f32[3,2,16,128]{3,2,1,0:T(8,128)S(1)} %get-tuple-element.5), channel_id=1, source_target_pairs={{0,16},{16,32},{32,48},{48,64},{64,80},{80,96},{96,112},{112,128},... | collective-permute-start | bytes 147464 | tf_op jit(solution)/shard_map/ppermute | solution.py:58
  30.9 3.6 %collective-permute-start.22 = (f32[2,32,2,128]{3,2,1,0:T(2,128)S(1)}, f32[2,32,2,128]{3,2,1,0:T(2,128)S(1)}, u32[]{:S(2)}, u32[]{:S(2)}) collective-permute-start(f32[2,32,2,128]{3,2,1,0:T(2,128)S(1)} %get-tuple-element.56), channel_id=1, source_target_pairs={{1,0},{2,1},{3,2},{4,3},{5,4},{6,5},{7,6},{8,7},{9,8},{10,9},{11,1... | collective-permute-start | bytes 196616 | tf_op jit(solution)/shard_map/ppermute | solution.py:55
  34.6 5.6 %collective-permute-start.20 = (f32[2,2,16,128]{3,2,1,0:T(8,128)S(1)}, f32[2,2,16,128]{3,2,1,0:T(8,128)S(1)}, u32[]{:S(2)}, u32[]{:S(2)}) collective-permute-start(f32[2,2,16,128]{3,2,1,0:T(8,128)S(1)} %get-tuple-element.53), channel_id=1, source_target_pairs={{0,16},{16,32},{32,48},{48,64},{64,80},{80,96},{96,112},{112,128},... | collective-permute-start | bytes 98312 | tf_op jit(solution)/shard_map/ppermute | solution.py:58
  44.6 3.6 %collective-permute-start.6 = (f32[3,32,2,128]{3,2,1,0:T(2,128)S(1)}, f32[3,32,2,128]{3,2,1,0:T(2,128)S(1)}, u32[]{:S(2)}, u32[]{:S(2)}) collective-permute-start(f32[3,32,2,128]{3,2,1,0:T(2,128)S(1)} %get-tuple-element.34), channel_id=1, source_target_pairs={{1,0},{2,1},{3,2},{4,3},{5,4},{6,5},{7,6},{8,7},{9,8},{10,9},{11,1... | collective-permute-start | bytes 294920 | tf_op jit(solution)/shard_map/ppermute | solution.py:55
  48.2 5.7 %collective-permute-start.4 = (f32[3,2,16,128]{3,2,1,0:T(8,128)S(1)}, f32[3,2,16,128]{3,2,1,0:T(8,128)S(1)}, u32[]{:S(2)}, u32[]{:S(2)}) collective-permute-start(f32[3,2,16,128]{3,2,1,0:T(8,128)S(1)} %get-tuple-element.31), channel_id=1, source_target_pairs={{0,16},{16,32},{32,48},{48,64},{64,80},{80,96},{96,112},{112,128},... | collective-permute-start | bytes 147464 | tf_op jit(solution)/shard_map/ppermute | solution.py:58
  67.1 5.8 %all-to-all-start.2 = ((f32[16,2,2,16,128]{4,3,2,1,0:T(8,128)}), f32[16,2,2,16,128]{4,3,2,1,0:T(8,128)S(1)}, u32[]{:S(2)}, u32[]{:S(2)}) async-start(f32[16,2,2,16,128]{4,3,2,1,0:T(8,128)} %constant_dynamic-update-slice_fusion.16), calls=%async_computation.2 | async-start | bytes 1048576 | tf_op jit(solution)/shard_map/all_to_all | solution.py:9
  87.2 5.6 %all-to-all-start = ((f32[16,3,2,16,128]{4,3,2,1,0:T(8,128)}), f32[16,3,2,16,128]{4,3,2,1,0:T(8,128)S(1)}, u32[]{:S(2)}, u32[]{:S(2)}) async-start(f32[16,3,2,16,128]{4,3,2,1,0:T(8,128)} %constant_dynamic-update-slice_fusion), calls=%async_computation | async-start | bytes 1572864 | tf_op jit(solution)/shard_map/all_to_all | solution.py:9
  98.8 14.1 %all-to-all-done = f32[16,3,2,16,128]{4,3,2,1,0:T(8,128)S(1)} async-done(((f32[16,3,2,16,128]{4,3,2,1,0:T(8,128)}), f32[16,3,2,16,128]{4,3,2,1,0:T(8,128)S(1)}, u32[]{:S(2)}, u32[]{:S(2)}) %all-to-all-start) | async-done | bytes 786464 | tf_op jit(solution)/shard_map/all_to_all | solution.py:9
  112.9 3.6 %all-to-all-start.3 = ((f32[2,2,256,128]{3,1,0,2:T(2,128)}), f32[2,2,256,128]{3,1,0,2:T(2,128)S(1)}, u32[]{:S(2)}, u32[]{:S(2)}) async-start(f32[2,2,256,128]{3,1,0,2:T(2,128)} %copy.50), calls=%async_computation.3 | async-start | bytes 1048576 | tf_op jit(solution)/shard_map/all_to_all | solution.py:86
  118.5 14.8 %all-to-all-done.3 = f32[2,2,256,128]{3,1,0,2:T(2,128)S(1)} async-done(((f32[2,2,256,128]{3,1,0,2:T(2,128)}), f32[2,2,256,128]{3,1,0,2:T(2,128)S(1)}, u32[]{:S(2)}, u32[]{:S(2)}) %all-to-all-start.3) | async-done | bytes 524320 | tf_op jit(solution)/shard_map/all_to_all | solution.py:86
  133.2 3.6 %all-to-all-start.1 = ((f32[3,2,256,128]{3,1,0,2:T(2,128)}), f32[3,2,256,128]{3,1,0,2:T(2,128)S(1)}, u32[]{:S(2)}, u32[]{:S(2)}) async-start(f32[3,2,256,128]{3,1,0,2:T(2,128)} %copy.46), calls=%async_computation.1 | async-start | bytes 1572864 | tf_op jit(solution)/shard_map/all_to_all | solution.py:86
  138.5 2.2 %collective-permute-start.26 = (f32[2,32,2,128]{3,2,1,0:T(2,128)S(1)}, f32[2,32,2,128]{3,2,1,0:T(2,128)S(1)}, u32[]{:S(2)}, u32[]{:S(2)}) collective-permute-start(f32[2,32,2,128]{3,2,1,0:T(2,128)S(1)} %get-tuple-element.50), channel_id=1, source_target_pairs={{1,0},{2,1},{3,2},{4,3},{5,4},{6,5},{7,6},{8,7},{9,8},{10,9},{11,1... | collective-permute-start | bytes 196616 | tf_op jit(solution)/shard_map/ppermute | solution.py:55
  140.7 9.8 %collective-permute-start.24 = (f32[2,2,16,128]{3,2,1,0:T(8,128)S(1)}, f32[2,2,16,128]{3,2,1,0:T(8,128)S(1)}, u32[]{:S(2)}, u32[]{:S(2)}) collective-permute-start(f32[2,2,16,128]{3,2,1,0:T(8,128)S(1)} %get-tuple-element.47), channel_id=1, source_target_pairs={{0,16},{16,32},{32,48},{48,64},{64,80},{80,96},{96,112},{112,128},... | collective-permute-start | bytes 98312 | tf_op jit(solution)/shard_map/ppermute | solution.py:58
  152.5 4.9 %collective-permute-done.27 = f32[2,2,16,128]{3,2,1,0:T(8,128)S(1)} collective-permute-done((f32[2,2,16,128]{3,2,1,0:T(8,128)S(1)}, f32[2,2,16,128]{3,2,1,0:T(8,128)S(1)}, u32[]{:S(2)}, u32[]{:S(2)}) %collective-permute-start.27) | collective-permute-done | bytes 32800 | tf_op jit(solution)/shard_map/ppermute | solution.py:61
  159.6 2.9 %collective-permute-start.30 = (f32[2,32,2,128]{3,2,1,0:T(2,128)S(1)}, f32[2,32,2,128]{3,2,1,0:T(2,128)S(1)}, u32[]{:S(2)}, u32[]{:S(2)}) collective-permute-start(f32[2,32,2,128]{3,2,1,0:T(2,128)S(1)} %get-tuple-element.46), channel_id=1, source_target_pairs={{1,0},{2,1},{3,2},{4,3},{5,4},{6,5},{7,6},{8,7},{9,8},{10,9},{11,1... | collective-permute-start | bytes 196616 | tf_op jit(solution)/shard_map/ppermute | solution.py:55
  162.5 10.2 %collective-permute-start.28 = (f32[2,2,16,128]{3,2,1,0:T(8,128)S(1)}, f32[2,2,16,128]{3,2,1,0:T(8,128)S(1)}, u32[]{:S(2)}, u32[]{:S(2)}) collective-permute-start(f32[2,2,16,128]{3,2,1,0:T(8,128)S(1)} %get-tuple-element.43), channel_id=1, source_target_pairs={{0,16},{16,32},{32,48},{48,64},{64,80},{80,96},{96,112},{112,128},... | collective-permute-start | bytes 98312 | tf_op jit(solution)/shard_map/ppermute | solution.py:58
  176.5 3.6 %collective-permute-done.31 = f32[2,2,16,128]{3,2,1,0:T(8,128)S(1)} collective-permute-done((f32[2,2,16,128]{3,2,1,0:T(8,128)S(1)}, f32[2,2,16,128]{3,2,1,0:T(8,128)S(1)}, u32[]{:S(2)}, u32[]{:S(2)}) %collective-permute-start.31) | collective-permute-done | bytes 32800 | tf_op jit(solution)/shard_map/ppermute | solution.py:61
  182.0 5.4 %collective-permute-start.8 = (f32[3,2,16,128]{3,2,1,0:T(8,128)S(1)}, f32[3,2,16,128]{3,2,1,0:T(8,128)S(1)}, u32[]{:S(2)}, u32[]{:S(2)}) collective-permute-start(f32[3,2,16,128]{3,2,1,0:T(8,128)S(1)} %get-tuple-element.25), channel_id=1, source_target_pairs={{0,16},{16,32},{32,48},{48,64},{64,80},{80,96},{96,112},{112,128},... | collective-permute-start | bytes 147464 | tf_op jit(solution)/shard_map/ppermute | solution.py:58
  190.9 3.6 %collective-permute-start.14 = (f32[3,32,2,128]{3,2,1,0:T(2,128)S(1)}, f32[3,32,2,128]{3,2,1,0:T(2,128)S(1)}, u32[]{:S(2)}, u32[]{:S(2)}) collective-permute-start(f32[3,32,2,128]{3,2,1,0:T(2,128)S(1)} %get-tuple-element.24), channel_id=1, source_target_pairs={{1,0},{2,1},{3,2},{4,3},{5,4},{6,5},{7,6},{8,7},{9,8},{10,9},{11,1... | collective-permute-start | bytes 294920 | tf_op jit(solution)/shard_map/ppermute | solution.py:55
  194.4 6.3 %collective-permute-start.12 = (f32[3,2,16,128]{3,2,1,0:T(8,128)S(1)}, f32[3,2,16,128]{3,2,1,0:T(8,128)S(1)}, u32[]{:S(2)}, u32[]{:S(2)}) collective-permute-start(f32[3,2,16,128]{3,2,1,0:T(8,128)S(1)} %get-tuple-element.21), channel_id=1, source_target_pairs={{0,16},{16,32},{32,48},{48,64},{64,80},{80,96},{96,112},{112,128},... | collective-permute-start | bytes 147464 | tf_op jit(solution)/shard_map/ppermute | solution.py:58
  204.0 3.7 %collective-permute-done.15 = f32[3,2,16,128]{3,2,1,0:T(8,128)S(1)} collective-permute-done((f32[3,2,16,128]{3,2,1,0:T(8,128)S(1)}, f32[3,2,16,128]{3,2,1,0:T(8,128)S(1)}, u32[]{:S(2)}, u32[]{:S(2)}) %collective-permute-start.15) | collective-permute-done | bytes 49184 | tf_op jit(solution)/shard_map/ppermute | solution.py:61
  (144 shorter events, 73.2 us)
Async XLA Ops:
  1.3 38.8 %collective-permute-start.1 = (f32[3,32,2,128]{3,2,1,0:T(2,128)S(1)}, f32[3,32,2,128]{3,2,1,0:T(2,128)S(1)}, u32[]{:S(2)}, u32[]{:S(2)}) collective-permute-start(f32[3,32,2,128]{3,2,1,0:T(2,128)S(1)} %get-tuple-element.7), channel_id=1, source_target_pairs={{0,1},{1,2},{2,3},{3,4},{4,5},{5,6},{6,7},{7,8},{8,9},{9,10},{10,1... | collective-permute-start | bytes 294920 | tf_op jit(solution)/shard_map/ppermute | solution.py:52
  4.6 22.8 %collective-permute-start.17 = (f32[2,32,2,128]{3,2,1,0:T(2,128)S(1)}, f32[2,32,2,128]{3,2,1,0:T(2,128)S(1)}, u32[]{:S(2)}, u32[]{:S(2)}) collective-permute-start(f32[2,32,2,128]{3,2,1,0:T(2,128)S(1)} %get-tuple-element.11), channel_id=1, source_target_pairs={{0,1},{1,2},{2,3},{3,4},{4,5},{5,6},{6,7},{7,8},{8,9},{9,10},{10,1... | collective-permute-start | bytes 196616 | tf_op jit(solution)/shard_map/ppermute | solution.py:52
  6.2 23.1 %collective-permute-start.18 = (f32[2,32,2,128]{3,2,1,0:T(2,128)S(1)}, f32[2,32,2,128]{3,2,1,0:T(2,128)S(1)}, u32[]{:S(2)}, u32[]{:S(2)}) collective-permute-start(f32[2,32,2,128]{3,2,1,0:T(2,128)S(1)} %get-tuple-element.12), channel_id=1, source_target_pairs={{1,0},{2,1},{3,2},{4,3},{5,4},{6,5},{7,6},{8,7},{9,8},{10,9},{11,1... | collective-permute-start | bytes 196616 | tf_op jit(solution)/shard_map/ppermute | solution.py:55
  20.1 22.0 %collective-permute-start.2 = (f32[3,32,2,128]{3,2,1,0:T(2,128)S(1)}, f32[3,32,2,128]{3,2,1,0:T(2,128)S(1)}, u32[]{:S(2)}, u32[]{:S(2)}) collective-permute-start(f32[3,32,2,128]{3,2,1,0:T(2,128)S(1)} %get-tuple-element.8), channel_id=1, source_target_pairs={{1,0},{2,1},{3,2},{4,3},{5,4},{6,5},{7,6},{8,7},{9,8},{10,9},{11,1... | collective-permute-start | bytes 294920 | tf_op jit(solution)/shard_map/ppermute | solution.py:55
  30.8 23.1 %collective-permute-start.21 = (f32[2,32,2,128]{3,2,1,0:T(2,128)S(1)}, f32[2,32,2,128]{3,2,1,0:T(2,128)S(1)}, u32[]{:S(2)}, u32[]{:S(2)}) collective-permute-start(f32[2,32,2,128]{3,2,1,0:T(2,128)S(1)} %get-tuple-element.55), channel_id=1, source_target_pairs={{0,1},{1,2},{2,3},{3,4},{4,5},{5,6},{6,7},{7,8},{8,9},{9,10},{10,1... | collective-permute-start | bytes 196616 | tf_op jit(solution)/shard_map/ppermute | solution.py:52
  30.9 25.0 %collective-permute-start.22 = (f32[2,32,2,128]{3,2,1,0:T(2,128)S(1)}, f32[2,32,2,128]{3,2,1,0:T(2,128)S(1)}, u32[]{:S(2)}, u32[]{:S(2)}) collective-permute-start(f32[2,32,2,128]{3,2,1,0:T(2,128)S(1)} %get-tuple-element.56), channel_id=1, source_target_pairs={{1,0},{2,1},{3,2},{4,3},{5,4},{6,5},{7,6},{8,7},{9,8},{10,9},{11,1... | collective-permute-start | bytes 196616 | tf_op jit(solution)/shard_map/ppermute | solution.py:55
  44.5 28.4 %collective-permute-start.5 = (f32[3,32,2,128]{3,2,1,0:T(2,128)S(1)}, f32[3,32,2,128]{3,2,1,0:T(2,128)S(1)}, u32[]{:S(2)}, u32[]{:S(2)}) collective-permute-start(f32[3,32,2,128]{3,2,1,0:T(2,128)S(1)} %get-tuple-element.33), channel_id=1, source_target_pairs={{0,1},{1,2},{2,3},{3,4},{4,5},{5,6},{6,7},{7,8},{8,9},{9,10},{10,1... | collective-permute-start | bytes 294920 | tf_op jit(solution)/shard_map/ppermute | solution.py:52
  44.6 28.3 %collective-permute-start.6 = (f32[3,32,2,128]{3,2,1,0:T(2,128)S(1)}, f32[3,32,2,128]{3,2,1,0:T(2,128)S(1)}, u32[]{:S(2)}, u32[]{:S(2)}) collective-permute-start(f32[3,32,2,128]{3,2,1,0:T(2,128)S(1)} %get-tuple-element.34), channel_id=1, source_target_pairs={{1,0},{2,1},{3,2},{4,3},{5,4},{6,5},{7,6},{8,7},{9,8},{10,9},{11,1... | collective-permute-start | bytes 294920 | tf_op jit(solution)/shard_map/ppermute | solution.py:55
  48.2 24.7 %collective-permute-start.4 = (f32[3,2,16,128]{3,2,1,0:T(8,128)S(1)}, f32[3,2,16,128]{3,2,1,0:T(8,128)S(1)}, u32[]{:S(2)}, u32[]{:S(2)}) collective-permute-start(f32[3,2,16,128]{3,2,1,0:T(8,128)S(1)} %get-tuple-element.31), channel_id=1, source_target_pairs={{0,16},{16,32},{32,48},{48,64},{64,80},{80,96},{96,112},{112,128},... | collective-permute-start | bytes 147464 | tf_op jit(solution)/shard_map/ppermute | solution.py:58
  53.9 19.0 %collective-permute-start.7 = (f32[3,2,16,128]{3,2,1,0:T(8,128)S(1)}, f32[3,2,16,128]{3,2,1,0:T(8,128)S(1)}, u32[]{:S(2)}, u32[]{:S(2)}) collective-permute-start(f32[3,2,16,128]{3,2,1,0:T(8,128)S(1)} %get-tuple-element.32), channel_id=1, source_target_pairs={{16,0},{32,16},{48,32},{64,48},{80,64},{96,80},{112,96},{128,112},... | collective-permute-start | bytes 147464 | tf_op jit(solution)/shard_map/ppermute | solution.py:61
  67.1 20.1 %all-to-all-start.2 = ((f32[16,2,2,16,128]{4,3,2,1,0:T(8,128)}), f32[16,2,2,16,128]{4,3,2,1,0:T(8,128)S(1)}, u32[]{:S(2)}, u32[]{:S(2)}) async-start(f32[16,2,2,16,128]{4,3,2,1,0:T(8,128)} %constant_dynamic-update-slice_fusion.16), calls=%async_computation.2 | async-start | bytes 1048576 | tf_op jit(solution)/shard_map/all_to_all | solution.py:9
  87.2 25.7 %all-to-all-start = ((f32[16,3,2,16,128]{4,3,2,1,0:T(8,128)}), f32[16,3,2,16,128]{4,3,2,1,0:T(8,128)S(1)}, u32[]{:S(2)}, u32[]{:S(2)}) async-start(f32[16,3,2,16,128]{4,3,2,1,0:T(8,128)} %constant_dynamic-update-slice_fusion), calls=%async_computation | async-start | bytes 1572864 | tf_op jit(solution)/shard_map/all_to_all | solution.py:9
  112.9 20.3 %all-to-all-start.3 = ((f32[2,2,256,128]{3,1,0,2:T(2,128)}), f32[2,2,256,128]{3,1,0,2:T(2,128)S(1)}, u32[]{:S(2)}, u32[]{:S(2)}) async-start(f32[2,2,256,128]{3,1,0,2:T(2,128)} %copy.50), calls=%async_computation.3 | async-start | bytes 1048576 | tf_op jit(solution)/shard_map/all_to_all | solution.py:86
  133.2 41.4 %all-to-all-start.1 = ((f32[3,2,256,128]{3,1,0,2:T(2,128)}), f32[3,2,256,128]{3,1,0,2:T(2,128)S(1)}, u32[]{:S(2)}, u32[]{:S(2)}) async-start(f32[3,2,256,128]{3,1,0,2:T(2,128)} %copy.46), calls=%async_computation.1 | async-start | bytes 1572864 | tf_op jit(solution)/shard_map/all_to_all | solution.py:86
  137.1 20.4 %collective-permute-start.25 = (f32[2,32,2,128]{3,2,1,0:T(2,128)S(1)}, f32[2,32,2,128]{3,2,1,0:T(2,128)S(1)}, u32[]{:S(2)}, u32[]{:S(2)}) collective-permute-start(f32[2,32,2,128]{3,2,1,0:T(2,128)S(1)} %get-tuple-element.49), channel_id=1, source_target_pairs={{0,1},{1,2},{2,3},{3,4},{4,5},{5,6},{6,7},{7,8},{8,9},{9,10},{10,1... | collective-permute-start | bytes 196616 | tf_op jit(solution)/shard_map/ppermute | solution.py:52
  138.5 18.9 %collective-permute-start.26 = (f32[2,32,2,128]{3,2,1,0:T(2,128)S(1)}, f32[2,32,2,128]{3,2,1,0:T(2,128)S(1)}, u32[]{:S(2)}, u32[]{:S(2)}) collective-permute-start(f32[2,32,2,128]{3,2,1,0:T(2,128)S(1)} %get-tuple-element.50), channel_id=1, source_target_pairs={{1,0},{2,1},{3,2},{4,3},{5,4},{6,5},{7,6},{8,7},{9,8},{10,9},{11,1... | collective-permute-start | bytes 196616 | tf_op jit(solution)/shard_map/ppermute | solution.py:55
  140.7 11.7 %collective-permute-start.24 = (f32[2,2,16,128]{3,2,1,0:T(8,128)S(1)}, f32[2,2,16,128]{3,2,1,0:T(8,128)S(1)}, u32[]{:S(2)}, u32[]{:S(2)}) collective-permute-start(f32[2,2,16,128]{3,2,1,0:T(8,128)S(1)} %get-tuple-element.47), channel_id=1, source_target_pairs={{0,16},{16,32},{32,48},{48,64},{64,80},{80,96},{96,112},{112,128},... | collective-permute-start | bytes 98312 | tf_op jit(solution)/shard_map/ppermute | solution.py:58
  158.9 23.1 %collective-permute-start.29 = (f32[2,32,2,128]{3,2,1,0:T(2,128)S(1)}, f32[2,32,2,128]{3,2,1,0:T(2,128)S(1)}, u32[]{:S(2)}, u32[]{:S(2)}) collective-permute-start(f32[2,32,2,128]{3,2,1,0:T(2,128)S(1)} %get-tuple-element.45), channel_id=1, source_target_pairs={{0,1},{1,2},{2,3},{3,4},{4,5},{5,6},{6,7},{7,8},{8,9},{9,10},{10,1... | collective-permute-start | bytes 196616 | tf_op jit(solution)/shard_map/ppermute | solution.py:52
  159.6 27.8 %collective-permute-start.30 = (f32[2,32,2,128]{3,2,1,0:T(2,128)S(1)}, f32[2,32,2,128]{3,2,1,0:T(2,128)S(1)}, u32[]{:S(2)}, u32[]{:S(2)}) collective-permute-start(f32[2,32,2,128]{3,2,1,0:T(2,128)S(1)} %get-tuple-element.46), channel_id=1, source_target_pairs={{1,0},{2,1},{3,2},{4,3},{5,4},{6,5},{7,6},{8,7},{9,8},{10,9},{11,1... | collective-permute-start | bytes 196616 | tf_op jit(solution)/shard_map/ppermute | solution.py:55
  162.5 12.5 %collective-permute-start.28 = (f32[2,2,16,128]{3,2,1,0:T(8,128)S(1)}, f32[2,2,16,128]{3,2,1,0:T(8,128)S(1)}, u32[]{:S(2)}, u32[]{:S(2)}) collective-permute-start(f32[2,2,16,128]{3,2,1,0:T(8,128)S(1)} %get-tuple-element.43), channel_id=1, source_target_pairs={{0,16},{16,32},{32,48},{48,64},{64,80},{80,96},{96,112},{112,128},... | collective-permute-start | bytes 98312 | tf_op jit(solution)/shard_map/ppermute | solution.py:58
  174.9 13.4 %collective-permute-start.10 = (f32[3,32,2,128]{3,2,1,0:T(2,128)S(1)}, f32[3,32,2,128]{3,2,1,0:T(2,128)S(1)}, u32[]{:S(2)}, u32[]{:S(2)}) collective-permute-start(f32[3,32,2,128]{3,2,1,0:T(2,128)S(1)} %get-tuple-element.28), channel_id=1, source_target_pairs={{1,0},{2,1},{3,2},{4,3},{5,4},{6,5},{7,6},{8,7},{9,8},{10,9},{11,1... | collective-permute-start | bytes 294920 | tf_op jit(solution)/shard_map/ppermute | solution.py:55
  175.0 13.3 %collective-permute-start.9 = (f32[3,32,2,128]{3,2,1,0:T(2,128)S(1)}, f32[3,32,2,128]{3,2,1,0:T(2,128)S(1)}, u32[]{:S(2)}, u32[]{:S(2)}) collective-permute-start(f32[3,32,2,128]{3,2,1,0:T(2,128)S(1)} %get-tuple-element.27), channel_id=1, source_target_pairs={{0,1},{1,2},{2,3},{3,4},{4,5},{5,6},{6,7},{7,8},{8,9},{9,10},{10,1... | collective-permute-start | bytes 294920 | tf_op jit(solution)/shard_map/ppermute | solution.py:52
  190.8 16.9 %collective-permute-start.13 = (f32[3,32,2,128]{3,2,1,0:T(2,128)S(1)}, f32[3,32,2,128]{3,2,1,0:T(2,128)S(1)}, u32[]{:S(2)}, u32[]{:S(2)}) collective-permute-start(f32[3,32,2,128]{3,2,1,0:T(2,128)S(1)} %get-tuple-element.23), channel_id=1, source_target_pairs={{0,1},{1,2},{2,3},{3,4},{4,5},{5,6},{6,7},{7,8},{8,9},{9,10},{10,1... | collective-permute-start | bytes 294920 | tf_op jit(solution)/shard_map/ppermute | solution.py:52
  190.9 16.8 %collective-permute-start.14 = (f32[3,32,2,128]{3,2,1,0:T(2,128)S(1)}, f32[3,32,2,128]{3,2,1,0:T(2,128)S(1)}, u32[]{:S(2)}, u32[]{:S(2)}) collective-permute-start(f32[3,32,2,128]{3,2,1,0:T(2,128)S(1)} %get-tuple-element.24), channel_id=1, source_target_pairs={{1,0},{2,1},{3,2},{4,3},{5,4},{6,5},{7,6},{8,7},{9,8},{10,9},{11,1... | collective-permute-start | bytes 294920 | tf_op jit(solution)/shard_map/ppermute | solution.py:55
  (16 other events, 166.8 us)
